TPU v7x, 128 devices: a whole 4x4x4 slice. The times are simulated.
128 devices in a mesh: blk: 16 (over x, y_hi, core), req: 8 (over y_lo, z).
Axes of the slice: x: 4, y: 4 (y_hi: 2, y_lo: 2; y = y_hi * 2 + y_lo), z: 4, core: 2. Of those that a mesh axis runs over, the one named last changes fastest.
Arguments:
- long_q: bfloat16 [16384, 2048], P('blk', 'req'), may hold values from -6 to 6
- long_k: bfloat16 [16384, 2048], P('blk', 'req'), may hold values from -6 to 6
- long_v: bfloat16 [16384, 2048], P('blk', 'req'), may hold values from -6 to 6
- short_q: bfloat16 [8192, 2048], P('blk', 'req'), may hold values from -6 to 6
- short_k: bfloat16 [8192, 2048], P('blk', 'req'), may hold values from -6 to 6
- short_v: bfloat16 [8192, 2048], P('blk', 'req'), may hold values from -6 to 6
- short_seg: int32 [16, 512], P('blk'), may hold values from 0 to 15, never falling along the last dimension, each value on 1 to 96 neighbouring positions
- pool_kv: bfloat16 [1024, 2, 16, 2048], P('blk', None, None, 'req'), may hold values from -6 to 6
- page_table: int32 [16, 16, 4], replicated, may hold values from 0 to 1023, as said below
- w_out: bfloat16 [2048, 2048], replicated, may hold values from -0.125 to 0.125
Outputs:
- long_out: bfloat16 [16384, 2048], P(('blk', 'req'))
- short_out: bfloat16 [8192, 2048], P(('blk', 'req'))
Inputs may be any that keep to these rules, and one draw needn't show every extreme that they name: `short_seg`: along each pack the request numbers never fall, and each of the 16 requests has 1 to 96 tokens, one of them exactly 96. `page_table`: entry [b, s, j] is o * 64 + i for page i of the pool rows held by index o of blk; for every pack b and every o exactly 4 of the 64 entries of b name pages of o.
All inputs are finite; a program needn't handle non-finite values.
Results may differ from a plain program's by a relative error of at most 0.015.
Values may be sent and summed in bfloat16 or wider, within the bound.
No kernel may reach another device: no remote copies, remote signals or barrier semaphores. Data moves between devices by JAX's collectives and lax.ppermute only.
A program may use at most 128 MiB of HBM per device.

v0:
```python
import math
import jax
import jax.numpy as jnp
from jax import lax
from jax.sharding import PartitionSpec as P

HD = 128
PPS = 4
very_negative = -1e30


def fold_block(state_now, query_heads, query_pos, key_block, value_block, block_first):
    acc_sum, run_max, run_total = state_now
    heads_dev = query_heads.shape[1]
    key_heads = key_block.reshape(key_block.shape[0], heads_dev, HD)
    value_heads = value_block.reshape(value_block.shape[0], heads_dev, HD)
    scores = jnp.einsum(
        "qhd,khd->hqk", query_heads, key_heads, preferred_element_type=jnp.float32
    ) * HD ** (-0.5)
    key_pos = block_first + jnp.arange(key_block.shape[0], dtype=jnp.int32)
    allowed = (key_pos[None, :] <= query_pos[:, None])[None]
    scores = jnp.where(allowed, scores, very_negative)
    new_max = jnp.maximum(run_max, jnp.max(scores, axis=-1))
    weights = jnp.where(allowed, jnp.exp(scores - new_max[..., None]), 0.0)
    factor = jnp.exp(run_max - new_max)
    run_total = run_total * factor + jnp.sum(weights, axis=-1)
    acc_sum = acc_sum * factor[..., None] + jnp.einsum(
        "hqk,khd->hqd",
        weights.astype(jnp.bfloat16),
        value_heads,
        preferred_element_type=jnp.float32,
    )
    return (acc_sum, new_max, run_total)


def prompt_attention(queries, query_pos, long_k, long_v):
    row_count, width = queries.shape
    heads_dev = width // HD
    query_heads = queries.reshape(row_count, heads_dev, HD)
    last_pos = jnp.max(query_pos)
    init = (
        jnp.zeros((heads_dev, row_count, HD), jnp.float32),
        jnp.full((heads_dev, row_count), very_negative, jnp.float32),
        jnp.zeros((heads_dev, row_count), jnp.float32),
    )
    key_piece = lax.all_gather(long_k, "blk", axis=0, tiled=True)
    value_piece = lax.all_gather(long_v, "blk", axis=0, tiled=True)
    piece_rows = key_piece.shape[0]
    step_rows = math.gcd(piece_rows, 1024)

    def one_step(block_num, state_in):
        block_start = block_num * step_rows
        key_block = lax.dynamic_slice_in_dim(key_piece, block_start, step_rows, 0)
        value_block = lax.dynamic_slice_in_dim(value_piece, block_start, step_rows, 0)

        def compute_block(state_live):
            return fold_block(
                state_live, query_heads, query_pos, key_block, value_block, block_start
            )

        def keep_state(state_skip):
            return state_skip

        return lax.cond(block_start <= last_pos, compute_block, keep_state, state_in)

    acc_sum, run_max, run_total = lax.fori_loop(0, piece_rows // step_rows, one_step, init)
    merged = acc_sum / run_total[..., None]
    return merged.transpose(1, 0, 2).reshape(row_count, width).astype(jnp.bfloat16)


def pack_attention(
    short_q, short_k, short_v, short_seg, pool_kv, page_table, block_index, block_count
):
    pack_rows, width = short_q.shape
    heads_dev = width // HD
    pool_pages = pool_kv.shape[0]
    page_len = pool_kv.shape[2]
    page_rows = page_table.reshape(block_count, -1)
    entries = page_rows.shape[1]
    capacity = entries // block_count
    owners = page_rows // pool_pages
    places = page_rows % pool_pages
    wanted = owners == block_index
    ranks = jnp.cumsum(wanted.astype(jnp.int32), axis=1) - 1
    picked = wanted[:, :, None] & (
        ranks[:, :, None] == jnp.arange(capacity, dtype=jnp.int32)[None, None, :]
    )
    send_places = jnp.sum(jnp.where(picked, places[:, :, None], 0), axis=1)
    outgoing = pool_kv[send_places.reshape(-1)].reshape(block_count, capacity, 2, page_len, width)
    arrived = lax.all_to_all(outgoing, "blk", split_axis=0, concat_axis=0, tiled=True)
    my_owners = lax.dynamic_index_in_dim(owners, block_index, 0, keepdims=False)
    order = jnp.arange(entries, dtype=jnp.int32)
    before = (my_owners[None, :] == my_owners[:, None]) & (order[None, :] < order[:, None])
    slots = my_owners * capacity + jnp.sum(before.astype(jnp.int32), axis=1)
    fetched = arrived.reshape(block_count * capacity, 2, page_len, width)[slots]
    cache_len = entries * page_len
    key_rows = jnp.concatenate([fetched[:, 0].reshape(cache_len, width), short_k], 0)
    value_rows = jnp.concatenate([fetched[:, 1].reshape(cache_len, width), short_v], 0)
    segment = short_seg[0]
    positions = jnp.arange(pack_rows, dtype=jnp.int32)
    key_seg = jnp.concatenate([jnp.arange(cache_len, dtype=jnp.int32) // (PPS * page_len), segment])
    key_pos = jnp.concatenate([jnp.full((cache_len,), -1, jnp.int32), positions])
    allowed = ((key_seg[None, :] == segment[:, None]) & (key_pos[None, :] <= positions[:, None]))[
        None
    ]
    query_heads = short_q.reshape(pack_rows, heads_dev, HD)
    key_heads = key_rows.reshape(cache_len + pack_rows, heads_dev, HD)
    value_heads = value_rows.reshape(cache_len + pack_rows, heads_dev, HD)
    scores = jnp.einsum(
        "qhd,khd->hqk", query_heads, key_heads, preferred_element_type=jnp.float32
    ) * HD ** (-0.5)
    scores = jnp.where(allowed, scores, very_negative)
    row_max = jnp.max(scores, axis=-1)
    weights = jnp.where(allowed, jnp.exp(scores - row_max[..., None]), 0.0)
    total = jnp.sum(weights, axis=-1)
    numer = jnp.einsum(
        "hqk,khd->hqd",
        weights.astype(jnp.bfloat16),
        value_heads,
        preferred_element_type=jnp.float32,
    )
    merged = numer / total[..., None]
    return merged.transpose(1, 0, 2).reshape(pack_rows, width).astype(jnp.bfloat16)


def per_device(
    long_q, long_k, long_v, short_q, short_k, short_v, short_seg, pool_kv, page_table, w_out
):
    block_count = lax.axis_size("blk")
    block_index = lax.axis_index("blk")
    group_index = lax.axis_index("req")
    row_count, width = long_q.shape
    query_pos = block_index * row_count + jnp.arange(row_count, dtype=jnp.int32)
    long_attn = prompt_attention(long_q, query_pos, long_k, long_v)
    short_attn = pack_attention(
        short_q, short_k, short_v, short_seg, pool_kv, page_table, block_index, block_count
    )
    w_rows = lax.dynamic_slice_in_dim(w_out, group_index * width, width, 0)
    long_out = lax.psum_scatter(
        jnp.dot(long_attn, w_rows, preferred_element_type=jnp.float32).astype(jnp.bfloat16),
        "req",
        scatter_dimension=0,
        tiled=True,
    )
    short_out = lax.psum_scatter(
        jnp.dot(short_attn, w_rows, preferred_element_type=jnp.float32).astype(jnp.bfloat16),
        "req",
        scatter_dimension=0,
        tiled=True,
    )
    return (long_out, short_out)


def solution(mesh):
    placed = (
        P("blk", "req"),
        P("blk", "req"),
        P("blk", "req"),
        P("blk", "req"),
        P("blk", "req"),
        P("blk", "req"),
        P("blk", None),
        P("blk", None, None, "req"),
        P(),
        P(),
    )
    return jax.shard_map(
        per_device,
        mesh=mesh,
        in_specs=placed,
        out_specs=(P(("blk", "req"), None), P(("blk", "req"), None)),
        check_vma=False,
    )
```

profile of v0, /device:TPU:1, one launch (start us, length us, event | category | flops | bytes accessed | tf_op | source)
XLA Modules:
  0.0 403.9 jit_solution(17348322285215755611)
XLA Ops:
  8.1 2.1 copy.40
  10.3 2.1 copy.42
  12.4 0.8 copy.45
  13.3 0.2 reduce_window_sum.11
  13.6 0.1 select_reduce_fusion
  13.7 0.1 copy.50
  13.8 0.1 reshape.279
  13.9 1.6 gather_fusion
  15.5 8.4 %all-to-all-start = ((bf16[16,4,2,16,256]{4,3,2,1,0:T(8,128)(2,1)}), bf16[16,4,2,16,256]{4,3,2,1,0:T(8,128)(2,1)S(1)}, u32[]{:S(2)}, u32[]{:S(2)}) async-start(bf16[16,4,2,16,256]{4,3,2,1,0:T(8,128)(2,1)} %bitcast.9), calls=%async_computation.1 | async-start | bytes 2097152 | tf_op jit(solution)/shard_map/all_to_all | solution.py:90
  24.0 0.1 copy.51
  24.2 0.8 copy.53
  25.0 0.1 copy.55
  25.2 0.2 convert_reduce_fusion
  25.4 1.9 fusion.20
  27.3 17.5 %all-to-all-done = bf16[16,4,2,16,256]{4,3,2,1,0:T(8,128)(2,1)S(1)} async-done(((bf16[16,4,2,16,256]{4,3,2,1,0:T(8,128)(2,1)}), bf16[16,4,2,16,256]{4,3,2,1,0:T(8,128)(2,1)S(1)}, u32[]{:S(2)}, u32[]{:S(2)}) %all-to-all-start) | async-done | bytes 1048608 | tf_op jit(solution)/shard_map/all_to_all | solution.py:90
  44.8 0.6 gather_fusion.1
  45.4 0.9 fusion.64
  46.3 1.2 concatenate.21
  47.5 0.1 copy.52
  47.5 0.1 concatenate.24
  47.7 0.4 copy.56
  48.1 6.6 %fusion.65 = (f32[2,512]{1,0:T(2,128)S(1)}, bf16[2,512,1536]{1,2,0:T(8,128)(2,1)}) fusion(pred[512,1536]{0,1:T(8,128)(4,1)} %fusion.20, bf16[512,2,128]{2,0,1:T(8,128)(2,1)} %copy.53, bf16[1024,2,128]{2,0,1:T(8,128)(2,1)S(1)} %copy.52, bf16[512,256]{1,0:T(8,128)(2,1)} %param.17), kind=kOutput, calls=%fused_computation.93 | convolution fusion | flops 413664768 | bytes 4984832 | tf_op jit(solution)/shard_map/sub | solution.py:114
  54.7 2.5 fusion.28
  57.2 3.3 convolution_convert_fusion.1
  60.6 0.2 reduce-scatter.3.cloned.1.call-start
  60.8 0.6 add_reduce_fusion
  61.4 0.2 copy.41
  61.7 0.3 copy.43
  61.9 35.7 %all-gather.3.cloned.1.call-done = bf16[16384,256]{0,1:T(8,128)(2,1)} async-done(((bf16[1024,256]{0,1:T(8,128)(2,1)}), bf16[16384,256]{0,1:T(8,128)(2,1)}) %all-gather.3.cloned.1.call-update) | async-done | bytes 8388624 | tf_op jit(solution)/shard_map/all_gather | solution.py:46
  97.6 73.6 %all-gather.5.cloned.1.call-done = bf16[16384,256]{0,1:T(8,128)(2,1)} async-done(((bf16[1024,256]{0,1:T(8,128)(2,1)}), bf16[16384,256]{0,1:T(8,128)(2,1)}) %all-gather.5.cloned.1.call-update) | async-done | bytes 8388624 | tf_op jit(solution)/shard_map/all_gather | solution.py:47
  171.3 0.1 broadcast_in_dim.90
  171.4 30.6 %while.18 = (s32[]{:T(128)}, f32[2,1024,128]{2,1,0:T(8,128)S(1)}, f32[2,1024]{1,0:T(2,128)S(1)}, f32[2,1024]{1,0:T(2,128)S(1)}, s32[]{:T(128)}, /*index=5*/bf16[...) while((s32[]{:T(128)}, f32[2,1024,128]{2,1,0:T(8,128)S(1)}, ...), condition=%wide.region_6.7_spmd.clone, body=%wide.region_1.6_spmd.clone.sunk | while | flops 1102583808 | bytes 35283264 | solution.py:66
  172.0 10.0 %conditional.3 = ((f32[2,1024,128]{2,1,0:T(8,128)S(1)}, f32[2,1024]{1,0:T(2,128)S(1)}, f32[2,1024]{1,0:T(2,128)S(1)})) conditional(s32[]{:T(128)} %convert_element_type.77, (f32[2,1024,128]{2,1,0:T(8,128)S(1)}, f32[2,1024]{1,0:T(2,128)S(1)}, f32[2,1024]{1,0:T(2,128)S(1)}) %tuple.66, (s32[]{:T(128)}, s32[]{:T(128)}, bf16[16384,256]{0,1:T(8,128)(2,1)}, ...), branch_computations={%region_2.0_spmd, %region_3.5_spmd} | conditional | flops 1102583808 | bytes 35278928 | solution.py:64
  172.0 1.3 constant_dynamic-slice_fusion
  173.3 0.7 broadcast_compare_fusion
  174.0 2.0 fusion.2
  176.0 2.3 fusion.3
  178.3 3.7 fusion.8
  182.7 10.0 %conditional.3 = ((f32[2,1024,128]{2,1,0:T(8,128)S(1)}, f32[2,1024]{1,0:T(2,128)S(1)}, f32[2,1024]{1,0:T(2,128)S(1)})) conditional(s32[]{:T(128)} %convert_element_type.77, (f32[2,1024,128]{2,1,0:T(8,128)S(1)}, f32[2,1024]{1,0:T(2,128)S(1)}, f32[2,1024]{1,0:T(2,128)S(1)}) %tuple.66, (s32[]{:T(128)}, s32[]{:T(128)}, bf16[16384,256]{0,1:T(8,128)(2,1)}, ...), branch_computations={%region_2.0_spmd, %region_3.5_spmd} | conditional | flops 1102583808 | bytes 35278928 | solution.py:64
  182.7 1.3 constant_dynamic-slice_fusion
  184.0 0.7 broadcast_compare_fusion
  184.6 2.0 fusion.2
  186.6 2.3 fusion.3
  188.9 3.7 fusion.8
  202.0 0.3 copy.44
  202.4 0.1 divide_convert_fusion
  202.5 4.5 %convolution_convert_fusion = bf16[1024,2048]{1,0:T(8,128)(2,1)} fusion(bf16[1024,256]{0,1:T(8,128)(2,1)S(1)} %bitcast.78, bf16[2048,2048]{1,0:T(8,128)(2,1)} %param.23, s32[]{:T(128)S(6)} %select_n.90), kind=kOutput, calls=%fused_computation.25 | convolution fusion | flops 1075838976 | bytes 5767172 | tf_op jit(solution)/shard_map/dot_general | solution.py:140
  207.0 189.5 %reduce-scatter.3.cloned.1.call-done = bf16[128,2048]{1,0:T(8,128)(2,1)} async-done(((bf16[1024,2048]{1,0:T(8,128)(2,1)}), bf16[128,2048]{1,0:T(8,128)(2,1)}) %reduce-scatter.3.cloned.1.call-update) | async-done | bytes 524304 | tf_op jit(solution)/shard_map/reduce_scatter | solution.py:139
  (71 shorter events, 0.8 us)
Async XLA Ops:
  8.0 5.9 %copy-start = (bf16[64,2,16,256]{3,2,1,0:T(8,128)(2,1)S(1)}, bf16[64,2,16,256]{3,2,1,0:T(8,128)(2,1)}, u32[]{:S(2)}) copy-start(bf16[64,2,16,256]{3,2,1,0:T(8,128)(2,1)} %param.21) | copy-start | bytes 3145732
  8.0 17.4 %copy-start.4 = (s32[1536]{0:T(1024)S(1)}, s32[1536]{0:T(1024)}, u32[]{:S(2)}) copy-start(s32[1536]{0:T(1024)} %constant.138.clone.1) | copy-start | bytes 18436
  8.0 16.0 %copy-start.2 = (bf16[512,256]{1,0:T(8,128)(2,1)S(1)}, bf16[512,256]{1,0:T(8,128)(2,1)}, u32[]{:S(2)}) copy-start(bf16[512,256]{1,0:T(8,128)(2,1)} %param.18) | copy-start | bytes 786436
  8.0 17.0 %copy-start.3 = (bf16[512,256]{1,0:T(8,128)(2,1)S(1)}, bf16[512,256]{1,0:T(8,128)(2,1)}, u32[]{:S(2)}) copy-start(bf16[512,256]{1,0:T(8,128)(2,1)} %param.19) | copy-start | bytes 786436
  8.0 17.4 %copy-start.5 = (s32[1,512]{1,0:T(1,128)S(1)}, s32[1,512]{1,0:T(1,128)}, u32[]{:S(2)}) copy-start(s32[1,512]{1,0:T(1,128)} %param.20) | copy-start | bytes 6148
  8.1 89.6 %all-gather.3.cloned.1.call-start = ((), (), s32[]{:S(2)}) async-start(), calls=%async_computation.3 | async-start | bytes 8912896 | tf_op jit(solution)/shard_map/all_gather | solution.py:46
  10.3 161.0 %all-gather.5.cloned.1.call-start = ((), (), s32[]{:S(2)}) async-start(), calls=%async_computation.4 | async-start | bytes 8912896 | tf_op jit(solution)/shard_map/all_gather | solution.py:47
  15.5 29.3 %all-to-all-start = ((bf16[16,4,2,16,256]{4,3,2,1,0:T(8,128)(2,1)}), bf16[16,4,2,16,256]{4,3,2,1,0:T(8,128)(2,1)S(1)}, u32[]{:S(2)}, u32[]{:S(2)}) async-start(bf16[16,4,2,16,256]{4,3,2,1,0:T(8,128)(2,1)} %bitcast.9), calls=%async_computation.1 | async-start | bytes 2097152 | tf_op jit(solution)/shard_map/all_to_all | solution.py:90
  24.0 183.0 %reduce-scatter.5.cloned.1.call-start = ((), (), s32[]{:S(2)}) async-start(), calls=%async_computation.6 | async-start | bytes 2359296 | tf_op jit(solution)/shard_map/reduce_scatter | solution.py:145
  54.7 6.8 %copy-start.1 = (bf16[1024,256]{1,0:T(8,128)(2,1)S(1)}, bf16[1024,256]{1,0:T(8,128)(2,1)}, u32[]{:S(2)}) copy-start(bf16[1024,256]{1,0:T(8,128)(2,1)} %param.14) | copy-start | bytes 1572868
  60.6 335.9 %reduce-scatter.3.cloned.1.call-start = ((), (), s32[]{:S(2)}) async-start(), calls=%async_computation.5 | async-start | bytes 4718592 | tf_op jit(solution)/shard_map/reduce_scatter | solution.py:139
Sparse Core Ops, SparseCore 0:
  11.9 85.6 all-gather.2
  100.1 71.1 all-gather.4
Sparse Core Ops, SparseCore 1:
  60.7 49.7 reduce-scatter.4
  207.1 189.4 reduce-scatter.2
where the time goes:
time: 405 us; the launch traced here: 404 us
  waiting for transfers between devices  316 us (78%)
  matrix products  28.3 us (7%)
  between operations  15.8 us (4%)
  local copies, waits for them, and re-layouts  14.8 us (4%)
  loops' own time  10.8 us (3%)
  other arithmetic  9.14 us (2%)
  starting transfers between devices  8.79 us (2%)
    reduce_scatter x1, waiting for transfers between devices, per_device(): lax.psum_scatter(jnp.dot(long_attn, w_rows, preferred_element_type=jnp.fl...  189 us
    all_gather x1, waiting for transfers between devices, prompt_attention(): value_piece = lax.all_gather(long_v, 'blk', axis=0, tiled=True)  73.6 us
    all_gather x1, waiting for transfers between devices, prompt_attention(): key_piece = lax.all_gather(long_k, 'blk', axis=0, tiled=True)  35.7 us
    all_to_all x1, waiting for transfers between devices, pack_attention(): lax.all_to_all(outgoing, 'blk', split_axis=0, concat_axis=0, tiled=True)  17.5 us
    another operation x1, loops' own time, prompt_attention(): lax.fori_loop(0, piece_rows // step_rows, one_step, init)  10.4 us
    all_to_all x1, starting transfers between devices, pack_attention(): lax.all_to_all(outgoing, 'blk', split_axis=0, concat_axis=0, tiled=True)  8.45 us
  transfers between devices with their start and end apart: 5, of which 4 were waited for; matrix products, arithmetic and copies ran while one was open for 12% of the time, Pallas kernels for 0%

commit v1 on v0

--- a/solution.py
+++ b/solution.py
@@ -43,8 +43,11 @@
         jnp.full((heads_dev, row_count), very_negative, jnp.float32),
         jnp.zeros((heads_dev, row_count), jnp.float32),
     )
-    key_piece = lax.all_gather(long_k, "blk", axis=0, tiled=True)
-    value_piece = lax.all_gather(long_v, "blk", axis=0, tiled=True)
+    key_piece, value_piece = jnp.split(
+        lax.all_gather(jnp.concatenate([long_k, long_v], axis=1), "blk", axis=0, tiled=True),
+        [long_k.shape[1]],
+        axis=1,
+    )
     piece_rows = key_piece.shape[0]
     step_rows = math.gcd(piece_rows, 1024)
 

time: 405 us -> 380 us (0.938)
  waiting for transfers between devices: 316 us -> 283 us
  local copies, waits for them, and re-layouts: 14.8 us -> 23.7 us
    all_gather x2 -> x1, waiting for transfers between devices: 109 us -> 74.8 us  [prompt_attention(): lax.all_gather(jnp.concatenate([long_k, long_v], axis=1), 'blk', axis=0,...]
    split x0 -> x1, local copies, waits for them, and re-layouts: none -> 11.5 us  [prompt_attention(): jnp.split(lax.all_gather(jnp.concatenate([long_k, long_v], axis=1), 'blk'...]
  transfers between devices with their start and end apart: 5 -> 4, of which waited for: 4 -> 3; matrix products, arithmetic and copies ran while one was open for 12% -> 15% of each run, Pallas kernels for 0% -> 0%
where the time goes in v1:
time: 380 us
  waiting for transfers between devices  283 us (74%)
  matrix products  27.8 us (7%)
  local copies, waits for them, and re-layouts  23.7 us (6%)
  between operations  15.8 us (4%)
  loops' own time  11 us (3%)
  other arithmetic  9.49 us (2%)
  starting transfers between devices  8.75 us (2%)
    reduce_scatter x1, waiting for transfers between devices, per_device(): lax.psum_scatter(jnp.dot(long_attn, w_rows, preferred_element_type=jnp.fl...  190 us
    all_gather x1, waiting for transfers between devices, prompt_attention(): lax.all_gather(jnp.concatenate([long_k, long_v], axis=1), 'blk', axis=0,...  74.8 us
    all_to_all x1, waiting for transfers between devices, pack_attention(): lax.all_to_all(outgoing, 'blk', split_axis=0, concat_axis=0, tiled=True)  18.6 us
    split x1, local copies, waits for them, and re-layouts, prompt_attention(): jnp.split(lax.all_gather(jnp.concatenate([long_k, long_v], axis=1), 'blk'...  11.5 us
    another operation x1, loops' own time, prompt_attention(): lax.fori_loop(0, piece_rows // step_rows, one_step, init)  10.7 us
    all_to_all x1, starting transfers between devices, pack_attention(): lax.all_to_all(outgoing, 'blk', split_axis=0, concat_axis=0, tiled=True)  8.45 us
  transfers between devices with their start and end apart: 4, of which 3 were waited for; matrix products, arithmetic and copies ran while one was open for 15% of the time, Pallas kernels for 0%

profile of v1, /device:TPU:1, one launch (start us, length us, event | category | flops | bytes accessed | tf_op | source)
XLA Modules:
  0.0 379.5 jit_solution(1840954491921131011)
XLA Ops:
  8.1 1.4 copy.40
  9.5 1.3 copy.41
  10.8 1.0 pad_maximum_fusion
  11.8 0.8 copy.45
  12.8 0.2 reduce_window_sum.11
  13.0 0.1 select_reduce_fusion
  13.2 0.1 copy.50
  13.2 0.1 reshape.279
  13.4 1.6 gather_fusion
  15.0 8.4 %all-to-all-start = ((bf16[16,4,2,16,256]{4,3,2,1,0:T(8,128)(2,1)}), bf16[16,4,2,16,256]{4,3,2,1,0:T(8,128)(2,1)S(1)}, u32[]{:S(2)}, u32[]{:S(2)}) async-start(bf16[16,4,2,16,256]{4,3,2,1,0:T(8,128)(2,1)} %bitcast.9), calls=%async_computation.1 | async-start | bytes 2097152 | tf_op jit(solution)/shard_map/all_to_all | solution.py:93
  23.5 0.1 copy.51
  23.6 0.8 copy.53
  24.5 0.8 copy.55
  25.3 0.7 add_reduce_fusion
  26.0 0.2 copy.42
  26.2 0.3 copy.43
  26.5 0.2 convert_reduce_fusion
  26.7 1.2 fusion.20
  27.9 18.6 %all-to-all-done = bf16[16,4,2,16,256]{4,3,2,1,0:T(8,128)(2,1)S(1)} async-done(((bf16[16,4,2,16,256]{4,3,2,1,0:T(8,128)(2,1)}), bf16[16,4,2,16,256]{4,3,2,1,0:T(8,128)(2,1)S(1)}, u32[]{:S(2)}, u32[]{:S(2)}) %all-to-all-start) | async-done | bytes 1048608 | tf_op jit(solution)/shard_map/all_to_all | solution.py:93
  46.5 0.6 gather_fusion.1
  47.1 0.1 fusion.65
  47.2 0.1 concatenate.25
  47.3 0.1 copy.52
  47.4 0.1 concatenate.28
  47.5 0.4 copy.56
  48.0 6.1 %fusion.66 = (f32[2,512]{1,0:T(2,128)S(1)}, bf16[2,512,1536]{1,2,0:T(8,128)(2,1)}) fusion(pred[512,1536]{0,1:T(8,128)(4,1)S(1)} %fusion.20, bf16[512,2,128]{2,0,1:T(8,128)(2,1)} %copy.53, bf16[1024,2,128]{2,0,1:T(8,128)(2,1)S(1)} %copy.52, bf16[512,256]{1,0:T(8,128)(2,1)} %param.17), kind=kOutput, calls=%fused_computation.95 | convolution fusion | flops 413664768 | bytes 4984832 | tf_op jit(solution)/shard_map/sub | solution.py:117
  54.1 2.5 fusion.28
  56.6 3.3 convolution_convert_fusion.1
  59.9 0.2 reduce-scatter.3.cloned.1.call-start
  60.1 74.8 %all-gather.2.cloned.1.call-done = bf16[16384,512]{0,1:T(8,128)(2,1)} async-done(((bf16[1024,512]{0,1:T(8,128)(2,1)}), bf16[16384,512]{0,1:T(8,128)(2,1)}) %all-gather.2.cloned.1.call-update) | async-done | bytes 16777232 | tf_op jit(solution)/shard_map/all_gather | solution.py:47
  134.9 11.5 %fusion.64 = (bf16[16384,256]{0,1:T(8,128)(2,1)}, bf16[16384,256]{0,1:T(8,128)(2,1)}) fusion(bf16[16384,512]{0,1:T(8,128)(2,1)} %all-gather.2.cloned.1.call-done), kind=kLoop, calls=%fused_computation.93 | loop fusion | bytes 33554432 | tf_op jit(solution)/shard_map/split | solution.py:46
  146.6 30.9 %while.18 = (s32[]{:T(128)}, f32[2,1024,128]{2,1,0:T(8,128)S(1)}, f32[2,1024]{1,0:T(2,128)S(1)}, f32[2,1024]{1,0:T(2,128)S(1)}, s32[]{:T(128)}, /*index=5*/bf16[...) while((s32[]{:T(128)}, f32[2,1024,128]{2,1,0:T(8,128)S(1)}, ...), condition=%wide.region_6.7_spmd.clone, body=%wide.region_1.6_spmd.clone.sunk | while | flops 1102583808 | bytes 35283256 | solution.py:69
  147.2 10.0 %conditional.3 = ((f32[2,1024,128]{2,1,0:T(8,128)S(1)}, f32[2,1024]{1,0:T(2,128)S(1)}, f32[2,1024]{1,0:T(2,128)S(1)})) conditional(s32[]{:T(128)} %convert_element_type.77, (f32[2,1024,128]{2,1,0:T(8,128)S(1)}, f32[2,1024]{1,0:T(2,128)S(1)}, f32[2,1024]{1,0:T(2,128)S(1)}) %tuple.67, (s32[]{:T(128)}, s32[]{:T(128)}, bf16[16384,256]{0,1:T(8,128)(2,1)}, ...), branch_computations={%region_2.0_spmd, %region_3.5_spmd} | conditional | flops 1102583808 | bytes 35278928 | solution.py:67
  147.3 0.7 broadcast_compare_fusion
  147.9 1.3 constant_dynamic-slice_fusion
  149.2 2.0 fusion.2
  151.2 2.3 fusion.3
  153.5 3.7 fusion.8
  157.9 10.0 %conditional.3 = ((f32[2,1024,128]{2,1,0:T(8,128)S(1)}, f32[2,1024]{1,0:T(2,128)S(1)}, f32[2,1024]{1,0:T(2,128)S(1)})) conditional(s32[]{:T(128)} %convert_element_type.77, (f32[2,1024,128]{2,1,0:T(8,128)S(1)}, f32[2,1024]{1,0:T(2,128)S(1)}, f32[2,1024]{1,0:T(2,128)S(1)}) %tuple.67, (s32[]{:T(128)}, s32[]{:T(128)}, bf16[16384,256]{0,1:T(8,128)(2,1)}, ...), branch_computations={%region_2.0_spmd, %region_3.5_spmd} | conditional | flops 1102583808 | bytes 35278928 | solution.py:67
  157.9 0.7 broadcast_compare_fusion
  158.6 1.3 constant_dynamic-slice_fusion
  159.9 2.0 fusion.2
  161.9 2.3 fusion.3
  164.1 3.7 fusion.8
  177.4 0.3 copy.44
  177.8 0.1 divide_convert_fusion
  177.9 4.5 %convolution_convert_fusion = bf16[1024,2048]{1,0:T(8,128)(2,1)} fusion(bf16[1024,256]{0,1:T(8,128)(2,1)S(1)} %bitcast.78, bf16[2048,2048]{1,0:T(8,128)(2,1)} %param.23, s32[]{:T(128)S(6)} %select_n.90), kind=kOutput, calls=%fused_computation.25 | convolution fusion | flops 1075838976 | bytes 5767172 | tf_op jit(solution)/shard_map/dot_general | solution.py:143
  182.5 189.6 %reduce-scatter.3.cloned.1.call-done = bf16[128,2048]{1,0:T(8,128)(2,1)} async-done(((bf16[1024,2048]{1,0:T(8,128)(2,1)}), bf16[128,2048]{1,0:T(8,128)(2,1)}) %reduce-scatter.3.cloned.1.call-update) | async-done | bytes 524304 | tf_op jit(solution)/shard_map/reduce_scatter | solution.py:142
  (74 shorter events, 0.7 us)
Async XLA Ops:
  8.0 5.4 %copy-start = (bf16[64,2,16,256]{3,2,1,0:T(8,128)(2,1)S(1)}, bf16[64,2,16,256]{3,2,1,0:T(8,128)(2,1)}, u32[]{:S(2)}) copy-start(bf16[64,2,16,256]{3,2,1,0:T(8,128)(2,1)} %param.21) | copy-start | bytes 3145732
  8.0 15.4 %copy-start.3 = (bf16[512,256]{1,0:T(8,128)(2,1)S(1)}, bf16[512,256]{1,0:T(8,128)(2,1)}, u32[]{:S(2)}) copy-start(bf16[512,256]{1,0:T(8,128)(2,1)} %param.18) | copy-start | bytes 786436
  8.0 16.4 %copy-start.4 = (bf16[512,256]{1,0:T(8,128)(2,1)S(1)}, bf16[512,256]{1,0:T(8,128)(2,1)}, u32[]{:S(2)}) copy-start(bf16[512,256]{1,0:T(8,128)(2,1)} %param.19) | copy-start | bytes 786436
  8.0 17.9 %copy-start.2 = (bf16[1024,256]{1,0:T(8,128)(2,1)S(1)}, bf16[1024,256]{1,0:T(8,128)(2,1)}, u32[]{:S(2)}) copy-start(bf16[1024,256]{1,0:T(8,128)(2,1)} %param.14) | copy-start | bytes 1572868
  8.0 126.9 %all-gather.2.cloned.1.call-start = ((), (), s32[]{:S(2)}) async-start(), calls=%async_computation.3 | async-start | bytes 17825792 | tf_op jit(solution)/shard_map/all_gather | solution.py:47
  9.5 17.2 %copy-start.7 = (s32[1,512]{1,0:T(1,128)S(1)}, s32[1,512]{1,0:T(1,128)}, u32[]{:S(2)}) copy-start(s32[1,512]{1,0:T(1,128)} %param.20) | copy-start | bytes 6148
  9.5 17.2 %copy-start.6 = (s32[1536]{0:T(1024)S(1)}, s32[1536]{0:T(1024)}, u32[]{:S(2)}) copy-start(s32[1536]{0:T(1024)} %constant.138.clone.1) | copy-start | bytes 18436
  15.0 31.5 %all-to-all-start = ((bf16[16,4,2,16,256]{4,3,2,1,0:T(8,128)(2,1)}), bf16[16,4,2,16,256]{4,3,2,1,0:T(8,128)(2,1)S(1)}, u32[]{:S(2)}, u32[]{:S(2)}) async-start(bf16[16,4,2,16,256]{4,3,2,1,0:T(8,128)(2,1)} %bitcast.9), calls=%async_computation.1 | async-start | bytes 2097152 | tf_op jit(solution)/shard_map/all_to_all | solution.py:93
  23.4 159.1 %reduce-scatter.5.cloned.1.call-start = ((), (), s32[]{:S(2)}) async-start(), calls=%async_computation.5 | async-start | bytes 2359296 | tf_op jit(solution)/shard_map/reduce_scatter | solution.py:148
  47.9 6.1 %copy-start.5 = (bf16[512,256]{0,1:T(8,128)(2,1)S(1)}, bf16[512,256]{0,1:T(8,128)(2,1)}, u32[]{:S(2)}) copy-start(bf16[512,256]{0,1:T(8,128)(2,1)} %copy.55) | copy-start | bytes 786436
  59.9 312.2 %reduce-scatter.3.cloned.1.call-start = ((), (), s32[]{:S(2)}) async-start(), calls=%async_computation.4 | async-start | bytes 4718592 | tf_op jit(solution)/shard_map/reduce_scatter | solution.py:142
  177.8 194.3 %copy-start.1 = (bf16[64,2,16,256]{3,2,1,0:T(8,128)(2,1)S(1)}, bf16[64,2,16,256]{3,2,1,0:T(8,128)(2,1)}, u32[]{:S(2)}) copy-start(bf16[64,2,16,256]{3,2,1,0:T(8,128)(2,1)} %param.21) | copy-start | bytes 3145732
Sparse Core Ops, SparseCore 0:
  12.0 122.9 all-gather.1
Sparse Core Ops, SparseCore 1:
  59.9 80.2 reduce-scatter.4
  182.6 189.5 reduce-scatter.2
